TPU v7x, 128 devices: a whole 4x4x4 slice. The times are simulated.
128 devices in a mesh: expert: 16 (over y, x), etp: 8 (over z, core).
Axes of the slice: x: 4, y: 4, z: 4, core: 2. Of those that a mesh axis runs over, the one named last changes fastest.
Arguments:
- tokens: bfloat16 [2048, 2048], P('expert'), may hold values from -6 to 6
- out_grad: bfloat16 [2048, 2048], P('expert'), may hold values from -6 to 6
- routes: int32 [2048, 2], P('expert'), may hold values from 0 to 15, as said below
- combine_weights: float32 [2048, 2], P('expert'), may hold values from 0.2 to 1
- w_gate: bfloat16 [16, 2048, 7168], P('expert', None, 'etp'), may hold values from -0.125 to 0.125
- w_up: bfloat16 [16, 2048, 7168], P('expert', None, 'etp'), may hold values from -0.125 to 0.125
- w_down: bfloat16 [16, 7168, 2048], P('expert', 'etp'), may hold values from -0.0625 to 0.0625
Outputs:
- mixed: bfloat16 [2048, 2048], P('expert')
- tokens_grad: bfloat16 [2048, 2048], P('expert')
- combine_grad: float32 [2048, 2], P('expert')
- gate_weight_grad: bfloat16 [16, 2048, 7168], P('expert', None, 'etp')
- up_weight_grad: bfloat16 [16, 2048, 7168], P('expert', None, 'etp')
- down_weight_grad: bfloat16 [16, 7168, 2048], P('expert', 'etp')
Inputs may be any that keep to these rules, and one draw needn't show every extreme that they name: `routes`: each token names two different experts. No expert is named by more than 32 tokens of one group of 128 consecutive tokens, and one expert, the same in every group, is named by exactly 32 tokens of each group.
All inputs are finite; a program needn't handle non-finite values.
Results may differ from a plain program's by a relative error of at most 0.02.
Values may be sent and summed in bfloat16 or wider, within the bound.
No kernel may reach another device: no remote copies, remote signals or barrier semaphores. Data moves between devices by JAX's collectives and lax.ppermute only.
A program may use at most 128 MiB of HBM per device.

v0:
```python
import jax
import jax.numpy as jnp
from jax import lax
from jax.sharding import PartitionSpec as P

TOP = 2


def slot_numbers(routes, expert_count):
    flattened = routes.reshape(-1)
    one_hot = (flattened[:, None] == jnp.arange(expert_count, dtype=jnp.int32)[None, :]).astype(
        jnp.int32
    )
    before = jnp.cumsum(one_hot, axis=0) - one_hot
    return jnp.sum(before * one_hot, axis=1).reshape(routes.shape)


def contract_last(left, right):
    return lax.dot_general(
        left, right, (((1,), (1,)), ((), ())), preferred_element_type=jnp.float32
    )


def contract_first(left, right):
    return lax.dot_general(
        left, right, (((0,), (0,)), ((), ())), preferred_element_type=jnp.float32
    )


def expert_pass(rows_in, rows_grad, gate_w, up_w, down_w):
    gate_pre = jnp.dot(rows_in, gate_w, preferred_element_type=jnp.float32)
    up_pre = jnp.dot(rows_in, up_w, preferred_element_type=jnp.float32)
    gate_sig = jax.nn.sigmoid(gate_pre)
    swish = gate_pre * gate_sig
    hidden = (swish * up_pre).astype(jnp.bfloat16)
    out_part = jnp.dot(hidden, down_w, preferred_element_type=jnp.float32)
    hidden_grad = contract_last(rows_grad, down_w)
    down_grad = contract_first(hidden, rows_grad).astype(jnp.bfloat16)
    gate_grad = (hidden_grad * up_pre * gate_sig * (1.0 + gate_pre * (1.0 - gate_sig))).astype(
        jnp.bfloat16
    )
    up_grad = (hidden_grad * swish).astype(jnp.bfloat16)
    gate_weight_grad = contract_first(rows_in, gate_grad).astype(jnp.bfloat16)
    up_weight_grad = contract_first(rows_in, up_grad).astype(jnp.bfloat16)
    input_part = contract_last(gate_grad, gate_w) + contract_last(up_grad, up_w)
    return (out_part, input_part, gate_weight_grad, up_weight_grad, down_grad)


def shards(tokens, out_grad, routes, combine_weights, w_gate, w_up, w_down):
    expert_count = lax.axis_size("expert")
    token_count, features = tokens.shape
    capacity = token_count // 4
    slots = slot_numbers(routes, expert_count)
    position = routes * capacity + slots
    pair_count = token_count * TOP
    source_index = jnp.full((expert_count * capacity,), pair_count, jnp.int32)
    source_index = source_index.at[position.reshape(-1)].set(
        jnp.arange(pair_count, dtype=jnp.int32)
    )
    zero_row = jnp.zeros((1, features), jnp.bfloat16)
    padded_tokens = jnp.concatenate([tokens, zero_row], axis=0)
    scaled_grad = (combine_weights[:, :, None] * out_grad[:, None, :]).astype(jnp.bfloat16)
    padded_grad = jnp.concatenate([scaled_grad.reshape(pair_count, features), zero_row], axis=0)
    send_rows = padded_tokens[source_index // TOP].reshape(expert_count, capacity, features)
    send_grad = padded_grad[source_index].reshape(expert_count, capacity, features)
    recv_rows, recv_grad = (
        lax.all_to_all(send_rows, "expert", split_axis=0, concat_axis=0, tiled=True),
        lax.all_to_all(send_grad, "expert", split_axis=0, concat_axis=0, tiled=True),
    )
    rows_in = recv_rows.reshape(expert_count * capacity, features)
    rows_grad = recv_grad.reshape(expert_count * capacity, features)
    out_part, input_part, gate_weight_grad, up_weight_grad, down_weight_grad = expert_pass(
        rows_in, rows_grad, w_gate[0], w_up[0], w_down[0]
    )
    out_part = out_part.reshape(expert_count, capacity, features)
    input_part = input_part.reshape(expert_count, capacity, features)
    grad_values = out_grad.astype(jnp.float32)
    out_sum, input_sum = (
        lax.psum(out_part.astype(jnp.bfloat16), "etp").astype(jnp.float32),
        lax.psum(input_part.astype(jnp.bfloat16), "etp").astype(jnp.float32),
    )
    out_back, input_back = (
        lax.all_to_all(
            out_sum.astype(jnp.bfloat16), "expert", split_axis=0, concat_axis=0, tiled=True
        ),
        lax.all_to_all(
            input_sum.astype(jnp.bfloat16), "expert", split_axis=0, concat_axis=0, tiled=True
        ),
    )
    out_pairs = out_back.reshape(expert_count * capacity, features)[position].astype(jnp.float32)
    input_pairs = input_back.reshape(expert_count * capacity, features)[position].astype(
        jnp.float32
    )
    mixed = jnp.sum(combine_weights[:, :, None] * out_pairs, axis=1).astype(jnp.bfloat16)
    combine_grad = jnp.sum(grad_values[:, None, :] * out_pairs, axis=2)
    tokens_grad = jnp.sum(input_pairs, axis=1).astype(jnp.bfloat16)
    return (
        mixed,
        tokens_grad,
        combine_grad,
        gate_weight_grad[None],
        up_weight_grad[None],
        down_weight_grad[None],
    )


def solution(mesh):
    return jax.shard_map(
        shards,
        mesh=mesh,
        in_specs=(
            P("expert", None),
            P("expert", None),
            P("expert", None),
            P("expert", None),
            P("expert", None, "etp"),
            P("expert", None, "etp"),
            P("expert", "etp", None),
        ),
        out_specs=(
            P("expert", None),
            P("expert", None),
            P("expert", None),
            P("expert", None, "etp"),
            P("expert", None, "etp"),
            P("expert", "etp", None),
        ),
        check_vma=False,
    )
```

profile of v0, /device:TPU:97, one launch (start us, length us, event | category | flops | bytes accessed | tf_op | source)
XLA Modules:
  0.0 264.5 jit_solution(16705591363725790153)
XLA Ops:
  7.2 0.8 copy.30
  10.4 1.4 scatter_custom_fusion
  11.8 1.1 concatenate.6
  12.9 3.3 %gather_fusion = bf16[512,2048]{1,0:T(8,128)(2,1)} fusion(bf16[129,2048]{1,0:T(8,128)(2,1)S(1)} %concatenate.6, s32[1024]{0:T(1024)S(1)} %get-tuple-element.30), kind=kCustom, calls=%fused_computation | custom fusion | bytes 4196352 | tf_op jit(solution)/shard_map/gather | solution.py:64
  16.2 6.9 %all-to-all-start = ((bf16[16,32,2048]{2,1,0:T(8,128)(2,1)}), bf16[16,32,2048]{2,1,0:T(8,128)(2,1)}, u32[]{:S(2)}, u32[]{:S(2)}) async-start(bf16[16,32,2048]{2,1,0:T(8,128)(2,1)} %bitcast.2), calls=%async_computation | async-start | bytes 4194304 | tf_op jit(solution)/shard_map/all_to_all | solution.py:67
  23.4 1.0 mul.71
  24.4 2.4 mul.72
  26.9 1.8 multiply_convert_fusion
  28.8 3.3 %gather_fusion.2 = bf16[512,2048]{1,0:T(8,128)(2,1)} fusion(bf16[257,2048]{1,0:T(8,128)(2,1)S(1)} %concatenate.7, s32[1024]{0:T(1024)S(1)} %get-tuple-element.29), kind=kCustom, calls=%fused_computation.2 | custom fusion | bytes 4196352 | tf_op jit(solution)/shard_map/gather | solution.py:65
  32.1 21.6 %all-to-all-done = bf16[16,32,2048]{2,1,0:T(8,128)(2,1)} async-done(((bf16[16,32,2048]{2,1,0:T(8,128)(2,1)}), bf16[16,32,2048]{2,1,0:T(8,128)(2,1)}, u32[]{:S(2)}, u32[]{:S(2)}) %all-to-all-start) | async-done | bytes 2097184 | tf_op jit(solution)/shard_map/all_to_all | solution.py:67
  53.7 4.3 %all-to-all-start.2 = ((bf16[16,32,2048]{2,1,0:T(8,128)(2,1)}), bf16[16,32,2048]{2,1,0:T(8,128)(2,1)S(1)}, u32[]{:S(2)}, u32[]{:S(2)}) async-start(bf16[16,32,2048]{2,1,0:T(8,128)(2,1)} %bitcast.10), calls=%async_computation.2 | async-start | bytes 4194304 | tf_op jit(solution)/shard_map/all_to_all | solution.py:68
  58.2 6.2 %fusion.6 = f32[512,896]{1,0:T(8,128)} fusion(bf16[512,2048]{1,0:T(8,128)(2,1)} %bitcast.3, bf16[1,2048,896]{2,1,0:T(8,128)(2,1)} %param.12), kind=kOutput, calls=%fused_computation.12 | convolution fusion | flops 1879048192 | bytes 7602176 | tf_op jit(solution)/shard_map/dot_general | solution.py:32
  64.4 22.3 %all-to-all-done.2 = bf16[16,32,2048]{2,1,0:T(8,128)(2,1)S(1)} async-done(((bf16[16,32,2048]{2,1,0:T(8,128)(2,1)}), bf16[16,32,2048]{2,1,0:T(8,128)(2,1)S(1)}, u32[]{:S(2)}, u32[]{:S(2)}) %all-to-all-start.2) | async-done | bytes 2097184 | tf_op jit(solution)/shard_map/all_to_all | solution.py:68
  86.7 5.2 %fusion.2 = f32[512,896]{1,0:T(8,128)S(1)} fusion(bf16[512,2048]{1,0:T(8,128)(2,1)S(1)} %bitcast.70, bf16[1,896,2048]{2,1,0:T(8,128)(2,1)} %param.13), kind=kOutput, calls=%fused_computation.8 | convolution fusion | flops 1879048192 | bytes 7602176 | tf_op jit(solution)/shard_map/dot_general | solution.py:19
  91.9 4.8 %multiply_convert_fusion.2 = (bf16[512,896]{1,0:T(8,128)(2,1)S(1)}, bf16[512,896]{1,0:T(8,128)(2,1)S(1)}, bf16[512,896]{1,0:T(8,128)(2,1)S(1)}) fusion(f32[512,896]{1,0:T(8,128)S(1)} %fusion.2, f32[512,896]{1,0:T(8,128)S(1)} %copy-done.12, bf16[512,2048]{1,0:T(8,128)(2,1)} %bitcast.3, bf16[1,2048,896]{2,1,0:T(8,128)(2,1)S(1)} %copy-done.6), kind=kOutput, calls=%fused_computation.26 | convolution fusion | flops 1885929472 | bytes 12189696 | tf_op jit(solution)/shard_map/dot_general | solution.py:31
  96.8 2.4 fusion.4
  99.8 3.7 %fusion.12 = bf16[16,32,2048]{2,1,0:T(8,128)(2,1)} fusion(bf16[16,32,896]{2,1,0:T(8,128)(2,1)S(1)} %bitcast.74, bf16[1,896,2048]{2,1,0:T(8,128)(2,1)S(1)} %copy-done.5), kind=kOutput, calls=%fused_computation.21 | convolution fusion | flops 1880096768 | bytes 6684672 | tf_op jit(solution)/shard_map/dot_general | solution.py:36
  103.4 3.7 %add_convert_fusion = bf16[512,2048]{1,0:T(8,128)(2,1)} fusion(f32[512,2048]{1,0:T(8,128)S(1)} %fusion.4, bf16[512,896]{1,0:T(8,128)(2,1)S(1)} %get-tuple-element.24, bf16[1,2048,896]{2,1,0:T(8,128)(2,1)S(1)} %copy-done.6), kind=kOutput, calls=%fused_computation.5 | convolution fusion | flops 1881145344 | bytes 10878976 | tf_op jit(solution)/shard_map/dot_general | solution.py:19
  107.1 72.5 %all-reduce.5.cloned.1.call-done = (bf16[16,32,2048]{2,1,0:T(8,128)(2,1)}, bf16[16,32,2048]{2,1,0:T(8,128)(2,1)}) async-done(((bf16[16,32,2048]{2,1,0:T(8,128)(2,1)}, bf16[16,32,2048]{2,1,0:T(8,128)(2,1)}), (bf16[16,32,2048]{2,1,0:T(8,128)(2,1)}, bf16[16,32,2048]{2,1,0:T(8,128)(2,1)})) %all-reduce.5.cloned.1.call-update) | async-done | bytes 4194320 | tf_op jit(solution)/shard_map/psum | solution.py:79
  179.6 34.4 %all_to_all.20 = bf16[16,32,2048]{2,1,0:T(8,128)(2,1)} all-to-all(bf16[16,32,2048]{2,1,0:T(8,128)(2,1)} %get-tuple-element.20), channel_id=1, replica_groups=mesh['expert'=16,'etp'=8] {'expert'}, dimensions={0} | all-to-all | bytes 4194304 | tf_op jit(solution)/shard_map/all_to_all | solution.py:83
  214.0 3.9 %all-to-all-start.3 = ((bf16[16,32,2048]{2,1,0:T(8,128)(2,1)}), bf16[16,32,2048]{2,1,0:T(8,128)(2,1)S(1)}, u32[]{:S(2)}, u32[]{:S(2)}) async-start(bf16[16,32,2048]{2,1,0:T(8,128)(2,1)} %get-tuple-element.21), calls=%async_computation.3 | async-start | bytes 4194304 | tf_op jit(solution)/shard_map/all_to_all | solution.py:86
  217.9 1.2 convert_element_type.61
  219.3 6.1 %convert_bitcast_fusion.1 = bf16[1,2048,896]{2,1,0:T(8,128)(2,1)} fusion(bf16[512,2048]{1,0:T(8,128)(2,1)} %bitcast.3, bf16[512,896]{1,0:T(8,128)(2,1)} %copy-done.9), kind=kOutput, calls=%fused_computation.19 | convolution fusion | flops 1880883200 | bytes 6684672 | tf_op jit(solution)/shard_map/dot_general | solution.py:25
  225.5 6.0 %convert_bitcast_fusion.2 = bf16[1,2048,896]{2,1,0:T(8,128)(2,1)} fusion(bf16[512,2048]{1,0:T(8,128)(2,1)} %bitcast.3, bf16[512,896]{1,0:T(8,128)(2,1)S(1)} %copy-done.11), kind=kOutput, calls=%fused_computation.20 | convolution fusion | flops 1880883200 | bytes 6684672 | tf_op jit(solution)/shard_map/dot_general | solution.py:25
  231.4 4.0 %convert_bitcast_fusion = bf16[1,896,2048]{2,1,0:T(8,128)(2,1)} fusion(bf16[512,896]{1,0:T(8,128)(2,1)S(1)} %copy-done.8, bf16[512,2048]{1,0:T(8,128)(2,1)S(1)} %bitcast.71), kind=kOutput, calls=%fused_computation.18 | convolution fusion | flops 1880883200 | bytes 6684672 | tf_op jit(solution)/shard_map/dot_general | solution.py:25
  235.4 4.2 %gather_fusion.1 = bf16[256,2048]{1,0:T(8,128)(2,1)S(1)} fusion(bf16[512,2048]{1,0:T(8,128)(2,1)} %bitcast.69, s32[1024]{0:T(1024)S(1)} %pad_clamp_fusion.1), kind=kCustom, calls=%fused_computation.1 | custom fusion | bytes 2098176 | tf_op jit(solution)/shard_map/gather | solution.py:90
  239.6 2.3 reshape.147
  241.9 6.5 %multiply_reduce_fusion = (f32[128,2]{1,0:T(8,128)S(1)}, bf16[128,2048]{1,0:T(8,128)(2,1)}) fusion(f32[128,2,2048]{2,1,0:T(2,128)} %reshape.147, f32[128,2048]{1,0:T(8,128)} %convert_element_type.61, f32[128,2]{1,0:T(8,128)S(1)} %copy.29), kind=kLoop, calls=%fused_computation.22 | loop fusion | flops 1834752 | bytes 3672064 | tf_op jit(solution)/shard_map/reduce_sum | solution.py:95
  249.1 2.8 %all-to-all-done.3 = bf16[16,32,2048]{2,1,0:T(8,128)(2,1)S(1)} async-done(((bf16[16,32,2048]{2,1,0:T(8,128)(2,1)}), bf16[16,32,2048]{2,1,0:T(8,128)(2,1)S(1)}, u32[]{:S(2)}, u32[]{:S(2)}) %all-to-all-start.3) | async-done | bytes 2097184 | tf_op jit(solution)/shard_map/all_to_all | solution.py:86
  251.9 1.4 gather_fusion.3
  253.3 0.7 reshape.130
  254.0 3.6 %reduce_sum.41 = bf16[128,2048]{1,0:T(8,128)(2,1)} reduce(bf16[128,2,2048]{2,1,0:T(2,128)(2,1)S(1)} %reshape.130, bf16[]{:T(256)} %constant.12.clone.1), dimensions={1}, to_apply=%region_7.8 | reduce | flops 262144 | bytes 1572866 | tf_op jit(solution)/shard_map/reduce_sum | solution.py:96
  (52 shorter events, 4.5 us)
Async XLA Ops:
  16.2 7.0 %copy-start.3 = (f32[128,2]{0,1:T(2,128)S(1)}, f32[128,2]{0,1:T(2,128)}, u32[]{:S(2)}) copy-start(f32[128,2]{0,1:T(2,128)} %param.10) | copy-start | bytes 3076
  16.2 7.2 %copy-start = (bf16[128,2048]{1,0:T(8,128)(2,1)S(1)}, bf16[128,2048]{1,0:T(8,128)(2,1)}, u32[]{:S(2)}) copy-start(bf16[128,2048]{1,0:T(8,128)(2,1)} %param.8) | copy-start | bytes 1572868
  16.2 37.5 %all-to-all-start = ((bf16[16,32,2048]{2,1,0:T(8,128)(2,1)}), bf16[16,32,2048]{2,1,0:T(8,128)(2,1)}, u32[]{:S(2)}, u32[]{:S(2)}) async-start(bf16[16,32,2048]{2,1,0:T(8,128)(2,1)} %bitcast.2), calls=%async_computation | async-start | bytes 4194304 | tf_op jit(solution)/shard_map/all_to_all | solution.py:67
  53.7 33.0 %all-to-all-start.2 = ((bf16[16,32,2048]{2,1,0:T(8,128)(2,1)}), bf16[16,32,2048]{2,1,0:T(8,128)(2,1)S(1)}, u32[]{:S(2)}, u32[]{:S(2)}) async-start(bf16[16,32,2048]{2,1,0:T(8,128)(2,1)} %bitcast.10), calls=%async_computation.2 | async-start | bytes 4194304 | tf_op jit(solution)/shard_map/all_to_all | solution.py:68
  57.9 121.7 %all-reduce.5.cloned.1.call-start = ((), (), s32[]{:S(2)}) async-start(), calls=%async_computation.4 | async-start | bytes 8388608 | tf_op jit(solution)/shard_map/psum | solution.py:79
  86.7 5.2 %copy-start.1 = (bf16[16,32,2048]{2,1,0:T(8,128)(2,1)}, bf16[16,32,2048]{2,1,0:T(8,128)(2,1)S(1)}, u32[]{:S(2)}) copy-start(bf16[16,32,2048]{2,1,0:T(8,128)(2,1)S(1)} %all-to-all-done.2) | copy-start | bytes 6291460
  86.7 5.2 %copy-start.6 = (bf16[1,2048,896]{2,1,0:T(8,128)(2,1)S(1)}, bf16[1,2048,896]{2,1,0:T(8,128)(2,1)}, u32[]{:S(2)}) copy-start(bf16[1,2048,896]{2,1,0:T(8,128)(2,1)} %param.11) | copy-start | bytes 11010052
  86.7 5.2 %copy-start.12 = (f32[512,896]{1,0:T(8,128)S(1)}, f32[512,896]{1,0:T(8,128)}, u32[]{:S(2)}) copy-start(f32[512,896]{1,0:T(8,128)} %fusion.6) | copy-start | bytes 5505028
  91.9 4.8 %copy-start.4 = (bf16[1,2048,896]{2,1,0:T(8,128)(2,1)S(1)}, bf16[1,2048,896]{2,1,0:T(8,128)(2,1)}, u32[]{:S(2)}) copy-start(bf16[1,2048,896]{2,1,0:T(8,128)(2,1)} %param.12) | copy-start | bytes 11010052
  96.7 2.4 copy-start.9
  96.7 2.4 copy-start.7
  96.7 6.7 %copy-start.10 = (bf16[512,896]{1,0:T(8,128)(2,1)}, bf16[512,896]{1,0:T(8,128)(2,1)S(1)}, u32[]{:S(2)}) copy-start(bf16[512,896]{1,0:T(8,128)(2,1)S(1)} %get-tuple-element.24) | copy-start | bytes 2752516
  96.8 3.0 %copy-start.5 = (bf16[1,896,2048]{2,1,0:T(8,128)(2,1)S(1)}, bf16[1,896,2048]{2,1,0:T(8,128)(2,1)}, u32[]{:S(2)}) copy-start(bf16[1,896,2048]{2,1,0:T(8,128)(2,1)} %param.13) | copy-start | bytes 11010052
  214.0 37.9 %all-to-all-start.3 = ((bf16[16,32,2048]{2,1,0:T(8,128)(2,1)}), bf16[16,32,2048]{2,1,0:T(8,128)(2,1)S(1)}, u32[]{:S(2)}, u32[]{:S(2)}) async-start(bf16[16,32,2048]{2,1,0:T(8,128)(2,1)} %get-tuple-element.21), calls=%async_computation.3 | async-start | bytes 4194304 | tf_op jit(solution)/shard_map/all_to_all | solution.py:86
  219.3 6.1 %copy-start.11 = (bf16[512,896]{1,0:T(8,128)(2,1)S(1)}, bf16[512,896]{1,0:T(8,128)(2,1)}, u32[]{:S(2)}) copy-start(bf16[512,896]{1,0:T(8,128)(2,1)} %copy-done.10) | copy-start | bytes 2752516
  225.4 6.0 %copy-start.2 = (bf16[16,32,2048]{2,1,0:T(8,128)(2,1)S(1)}, bf16[16,32,2048]{2,1,0:T(8,128)(2,1)}, u32[]{:S(2)}) copy-start(bf16[16,32,2048]{2,1,0:T(8,128)(2,1)} %copy-done.1) | copy-start | bytes 6291460
  225.5 6.0 %copy-start.8 = (bf16[512,896]{1,0:T(8,128)(2,1)S(1)}, bf16[512,896]{1,0:T(8,128)(2,1)}, u32[]{:S(2)}) copy-start(bf16[512,896]{1,0:T(8,128)(2,1)} %copy-done.7) | copy-start | bytes 2752516
Sparse Core Ops, SparseCore 0:
  107.3 72.3 all-reduce.4
where the time goes:
time: 265 us; the launch traced here: 264 us
  waiting for transfers between devices  119 us (45%)
  matrix products  42 us (16%)
  blocking collectives  34.4 us (13%)
  local copies, waits for them, and re-layouts  24.8 us (9%)
  starting transfers between devices  15.4 us (6%)
  other arithmetic  14.5 us (5%)
  between operations  14.3 us (5%)
    psum x1, waiting for transfers between devices, shards(): lax.psum(out_part.astype(jnp.bfloat16), 'etp').astype(jnp.float32)  72.5 us
    all_to_all x1, blocking collectives, shards(): lax.all_to_all(out_sum.astype(jnp.bfloat16), 'expert', split_axis=0, conc...  34.4 us
    all_to_all x1, waiting for transfers between devices, shards(): lax.all_to_all(send_grad, 'expert', split_axis=0, concat_axis=0, tiled=True)  22.3 us
    all_to_all x1, waiting for transfers between devices, shards(): lax.all_to_all(send_rows, 'expert', split_axis=0, concat_axis=0, tiled=True)  21.6 us
    dot_general x3, matrix products, contract_first(): lax.dot_general(left, right, (((0,), (0,)), ((), ())), preferred_element_...  16 us
    dot_general x3, matrix products, contract_last(): lax.dot_general(left, right, (((1,), (1,)), ((), ())), preferred_element_...  11.3 us
    all_to_all x1, starting transfers between devices, shards(): lax.all_to_all(send_rows, 'expert', split_axis=0, concat_axis=0, tiled=True)  6.94 us
    reduce_sum x1, other arithmetic, shards(): combine_grad = jnp.sum(grad_values[:, None, :] * out_pairs, axis=2)  6.54 us
  transfers between devices with their start and end apart: 4, of which 4 were waited for; matrix products, arithmetic and copies ran while one was open for 17% of the time, Pallas kernels for 0%

commit v1 on v0

--- a/solution.py
+++ b/solution.py
@@ -4,6 +4,12 @@
 from jax.sharding import PartitionSpec as P
 
 TOP = 2
+
+
+def summed_here(x, mesh_axis):
+    parts = lax.all_gather(x, mesh_axis, axis=0, tiled=False)
+    total = parts.sum(axis=0)
+    return total
 
 
 def slot_numbers(routes, expert_count):
@@ -76,7 +82,7 @@
     input_part = input_part.reshape(expert_count, capacity, features)
     grad_values = out_grad.astype(jnp.float32)
     out_sum, input_sum = (
-        lax.psum(out_part.astype(jnp.bfloat16), "etp").astype(jnp.float32),
+        summed_here(out_part.astype(jnp.bfloat16), "etp").astype(jnp.float32),
         lax.psum(input_part.astype(jnp.bfloat16), "etp").astype(jnp.float32),
     )
     out_back, input_back = (

time: 265 us -> 332 us (1.25); the launches traced: 264 us -> 328 us
  waiting for transfers between devices: 119 us -> 197 us
  blocking collectives: 34.4 us -> 0 us
  other arithmetic: 14.5 us -> 24 us
  starting transfers between devices: 15.4 us -> 24.9 us
    all_gather x0 -> x1, waiting for transfers between devices: none -> 79.9 us  [summed_here(): parts = lax.all_gather(x, mesh_axis, axis=0, tiled=False)]
    all_to_all x1 -> x0, blocking collectives: 34.4 us -> none  [shards(): lax.all_to_all(out_sum.astype(jnp.bfloat16), 'expert', split_axis=0, conc...]
    psum x1, waiting for transfers between devices: 72.5 us -> 60.5 us  [shards(): lax.psum(input_part.astype(jnp.bfloat16), 'etp').astype(jnp.float32)]
    reduce_sum x0 -> x1, other arithmetic: none -> 10.8 us  [summed_here(): total = parts.sum(axis=0)]
    all_to_all x0 -> x1, waiting for transfers between devices: none -> 9.27 us  [shards(): lax.all_to_all(out_sum.astype(jnp.bfloat16), 'expert', split_axis=0, conc...]
    all_to_all x0 -> x1, starting transfers between devices: none -> 6.96 us  [shards(): lax.all_to_all(out_sum.astype(jnp.bfloat16), 'expert', split_axis=0, conc...]
    all_to_all x1, waiting for transfers between devices: 22.3 us -> 26.1 us  [shards(): lax.all_to_all(send_grad, 'expert', split_axis=0, concat_axis=0, tiled=True)]
  transfers between devices with their start and end apart: 4 -> 6, of which waited for: 4 -> 5; matrix products, arithmetic and copies ran while one was open for 17% -> 15% of each run, Pallas kernels for 0% -> 0%
where the time goes in v1:
time: 332 us; the launch traced here: 328 us
  waiting for transfers between devices  197 us (59%)
  matrix products  43.4 us (13%)
  starting transfers between devices  24.9 us (8%)
  local copies, waits for them, and re-layouts  24.5 us (7%)
  other arithmetic  24 us (7%)
  between operations  14.4 us (4%)
    all_gather x1, waiting for transfers between devices, summed_here(): parts = lax.all_gather(x, mesh_axis, axis=0, tiled=False)  79.9 us
    psum x1, waiting for transfers between devices, shards(): lax.psum(input_part.astype(jnp.bfloat16), 'etp').astype(jnp.float32)  60.5 us
    all_to_all x1, waiting for transfers between devices, shards(): lax.all_to_all(send_grad, 'expert', split_axis=0, concat_axis=0, tiled=True)  26.1 us
    all_to_all x1, waiting for transfers between devices, shards(): lax.all_to_all(send_rows, 'expert', split_axis=0, concat_axis=0, tiled=True)  20.9 us
    dot_general x3, matrix products, contract_first(): lax.dot_general(left, right, (((0,), (0,)), ((), ())), preferred_element_...  16 us
    dot_general x3, matrix products, contract_last(): lax.dot_general(left, right, (((1,), (1,)), ((), ())), preferred_element_...  11.7 us
    reduce_sum x1, other arithmetic, summed_here(): total = parts.sum(axis=0)  10.8 us
    all_to_all x1, waiting for transfers between devices, shards(): lax.all_to_all(out_sum.astype(jnp.bfloat16), 'expert', split_axis=0, conc...  9.27 us
  transfers between devices with their start and end apart: 6, of which 5 were waited for; matrix products, arithmetic and copies ran while one was open for 15% of the time, Pallas kernels for 0%

profile of v1, /device:TPU:97, one launch (start us, length us, event | category | flops | bytes accessed | tf_op | source)
XLA Modules:
  0.0 327.9 jit_solution(12014203662124627781)
XLA Ops:
  8.2 2.1 mul.71
  10.4 2.4 mul.72
  14.5 1.4 scatter_custom_fusion
  15.9 1.8 multiply_convert_fusion
  17.8 3.3 %gather_fusion.2 = bf16[512,2048]{1,0:T(8,128)(2,1)} fusion(bf16[257,2048]{1,0:T(8,128)(2,1)S(1)} %concatenate.7, s32[1024]{0:T(1024)S(1)} %get-tuple-element.27), kind=kCustom, calls=%fused_computation.2 | custom fusion | bytes 4196352 | tf_op jit(solution)/shard_map/gather | solution.py:71
  21.1 6.8 %all-to-all-start.2 = ((bf16[16,32,2048]{2,1,0:T(8,128)(2,1)}), bf16[16,32,2048]{2,1,0:T(8,128)(2,1)S(1)}, u32[]{:S(2)}, u32[]{:S(2)}) async-start(bf16[16,32,2048]{2,1,0:T(8,128)(2,1)} %bitcast.11), calls=%async_computation.2 | async-start | bytes 4194304 | tf_op jit(solution)/shard_map/all_to_all | solution.py:74
  27.9 1.1 concatenate.6
  29.0 3.3 %gather_fusion = bf16[512,2048]{1,0:T(8,128)(2,1)} fusion(bf16[129,2048]{1,0:T(8,128)(2,1)S(1)} %concatenate.6, s32[1024]{0:T(1024)S(1)} %get-tuple-element.28), kind=kCustom, calls=%fused_computation | custom fusion | bytes 4196352 | tf_op jit(solution)/shard_map/gather | solution.py:70
  32.2 26.1 %all-to-all-done.2 = bf16[16,32,2048]{2,1,0:T(8,128)(2,1)S(1)} async-done(((bf16[16,32,2048]{2,1,0:T(8,128)(2,1)}), bf16[16,32,2048]{2,1,0:T(8,128)(2,1)S(1)}, u32[]{:S(2)}, u32[]{:S(2)}) %all-to-all-start.2) | async-done | bytes 2097184 | tf_op jit(solution)/shard_map/all_to_all | solution.py:74
  58.4 4.4 %all-to-all-start = ((bf16[16,32,2048]{2,1,0:T(8,128)(2,1)}), bf16[16,32,2048]{2,1,0:T(8,128)(2,1)}, u32[]{:S(2)}, u32[]{:S(2)}) async-start(bf16[16,32,2048]{2,1,0:T(8,128)(2,1)} %bitcast.2), calls=%async_computation | async-start | bytes 4194304 | tf_op jit(solution)/shard_map/all_to_all | solution.py:73
  63.1 5.6 %fusion.2 = f32[512,896]{1,0:T(8,128)} fusion(bf16[512,2048]{1,0:T(8,128)(2,1)S(1)} %bitcast.71, bf16[1,896,2048]{2,1,0:T(8,128)(2,1)} %param.13), kind=kOutput, calls=%fused_computation.8 | convolution fusion | flops 1879048192 | bytes 7602176 | tf_op jit(solution)/shard_map/dot_general | solution.py:25
  68.7 20.9 %all-to-all-done = bf16[16,32,2048]{2,1,0:T(8,128)(2,1)} async-done(((bf16[16,32,2048]{2,1,0:T(8,128)(2,1)}), bf16[16,32,2048]{2,1,0:T(8,128)(2,1)}, u32[]{:S(2)}, u32[]{:S(2)}) %all-to-all-start) | async-done | bytes 2097184 | tf_op jit(solution)/shard_map/all_to_all | solution.py:73
  89.5 5.1 %fusion.6 = f32[512,896]{1,0:T(8,128)S(1)} fusion(bf16[512,2048]{1,0:T(8,128)(2,1)} %bitcast.3, bf16[1,2048,896]{2,1,0:T(8,128)(2,1)} %param.12), kind=kOutput, calls=%fused_computation.12 | convolution fusion | flops 1879048192 | bytes 7602176 | tf_op jit(solution)/shard_map/dot_general | solution.py:38
  94.7 4.9 %multiply_convert_fusion.2 = (bf16[512,896]{1,0:T(8,128)(2,1)S(1)}, bf16[512,896]{1,0:T(8,128)(2,1)S(1)}, bf16[512,896]{1,0:T(8,128)(2,1)S(1)}) fusion(f32[512,896]{1,0:T(8,128)S(1)} %copy-done.11, f32[512,896]{1,0:T(8,128)S(1)} %fusion.6, bf16[512,2048]{1,0:T(8,128)(2,1)} %bitcast.3, bf16[1,2048,896]{2,1,0:T(8,128)(2,1)S(1)} %copy-done.6), kind=kOutput, calls=%fused_computation.26 | convolution fusion | flops 1885929472 | bytes 12189696 | tf_op jit(solution)/shard_map/dot_general | solution.py:37
  99.6 2.4 fusion.4
  102.0 3.7 %add_convert_fusion = bf16[512,2048]{1,0:T(8,128)(2,1)} fusion(f32[512,2048]{1,0:T(8,128)S(1)} %fusion.4, bf16[512,896]{1,0:T(8,128)(2,1)S(1)} %get-tuple-element.22, bf16[1,2048,896]{2,1,0:T(8,128)(2,1)S(1)} %copy-done.6), kind=kOutput, calls=%fused_computation.5 | convolution fusion | flops 1881145344 | bytes 10878976 | tf_op jit(solution)/shard_map/dot_general | solution.py:25
  105.8 5.7 %fusion.12 = bf16[16,32,2048]{2,1,0:T(8,128)(2,1)} fusion(bf16[16,32,896]{2,1,0:T(8,128)(2,1)S(1)} %bitcast.75, bf16[1,896,2048]{2,1,0:T(8,128)(2,1)} %param.13), kind=kOutput, calls=%fused_computation.21 | convolution fusion | flops 1880096768 | bytes 6684672 | tf_op jit(solution)/shard_map/dot_general | solution.py:42
  111.5 60.5 %all-reduce.4.cloned.1.call-done = bf16[16,32,2048]{2,1,0:T(8,128)(2,1)} async-done(((bf16[16,32,2048]{2,1,0:T(8,128)(2,1)}), bf16[16,32,2048]{2,1,0:T(8,128)(2,1)}) %all-reduce.4.cloned.1.call-update) | async-done | bytes 2097168 | tf_op jit(solution)/shard_map/psum | solution.py:86
  172.0 6.5 %all-to-all-start.3 = ((bf16[16,32,2048]{2,1,0:T(8,128)(2,1)}), bf16[16,32,2048]{2,1,0:T(8,128)(2,1)S(1)}, u32[]{:S(2)}, u32[]{:S(2)}) async-start(bf16[16,32,2048]{2,1,0:T(8,128)(2,1)} %all-reduce.4.cloned.1.call-done), calls=%async_computation.3 | async-start | bytes 4194304 | tf_op jit(solution)/shard_map/all_to_all | solution.py:92
  178.5 79.9 %all-gather.3.cloned.1.call-done = bf16[128,32,2048]{2,1,0:T(8,128)(2,1)} async-done(((bf16[16,32,2048]{2,1,0:T(8,128)(2,1)}), bf16[128,32,2048]{2,1,0:T(8,128)(2,1)}) %all-gather.3.cloned.1.call-update) | async-done | bytes 16777232 | tf_op jit(solution)/shard_map/all_gather | solution.py:10
  258.5 10.8 %reduce_sum.52 = bf16[16,32,2048]{2,1,0:T(8,128)(2,1)} reduce(bf16[8,16,32,2048]{3,2,1,0:T(8,128)(2,1)} %bitcast.70, bf16[]{:T(256)} %constant.13.clone.1), dimensions={0}, to_apply=%region_4.5 | reduce | flops 7340032 | bytes 18874370 | tf_op jit(solution)/shard_map/reduce_sum | solution.py:11
  269.2 7.0 %all-to-all-start.1 = ((bf16[16,32,2048]{2,1,0:T(8,128)(2,1)}), bf16[16,32,2048]{2,1,0:T(8,128)(2,1)}, u32[]{:S(2)}, u32[]{:S(2)}) async-start(bf16[16,32,2048]{2,1,0:T(8,128)(2,1)} %reduce_sum.52), calls=%async_computation.1 | async-start | bytes 4194304 | tf_op jit(solution)/shard_map/all_to_all | solution.py:89
  276.2 1.1 convert_element_type.63
  277.6 6.1 %convert_bitcast_fusion.2 = bf16[1,2048,896]{2,1,0:T(8,128)(2,1)} fusion(bf16[512,2048]{1,0:T(8,128)(2,1)} %bitcast.3, bf16[512,896]{1,0:T(8,128)(2,1)} %copy-done.12), kind=kOutput, calls=%fused_computation.20 | convolution fusion | flops 1880883200 | bytes 6684672 | tf_op jit(solution)/shard_map/dot_general | solution.py:31
  283.7 6.0 %convert_bitcast_fusion.1 = bf16[1,2048,896]{2,1,0:T(8,128)(2,1)} fusion(bf16[512,2048]{1,0:T(8,128)(2,1)} %bitcast.3, bf16[512,896]{1,0:T(8,128)(2,1)S(1)} %copy-done.10), kind=kOutput, calls=%fused_computation.19 | convolution fusion | flops 1880883200 | bytes 6684672 | tf_op jit(solution)/shard_map/dot_general | solution.py:31
  289.7 4.0 %convert_bitcast_fusion = bf16[1,896,2048]{2,1,0:T(8,128)(2,1)} fusion(bf16[512,896]{1,0:T(8,128)(2,1)S(1)} %copy-done.8, bf16[512,2048]{1,0:T(8,128)(2,1)S(1)} %bitcast.72), kind=kOutput, calls=%fused_computation.18 | convolution fusion | flops 1880883200 | bytes 6684672 | tf_op jit(solution)/shard_map/dot_general | solution.py:31
  293.6 1.4 gather_fusion.3
  296.0 3.6 %reduce_sum.54 = bf16[128,2048]{1,0:T(8,128)(2,1)} reduce(bf16[128,2,2048]{2,1,0:T(2,128)(2,1)S(1)} %reshape.130, bf16[]{:T(256)} %constant.13.clone.1), dimensions={1}, to_apply=%region_7.8 | reduce | flops 262144 | bytes 1572866 | tf_op jit(solution)/shard_map/reduce_sum | solution.py:102
  299.6 9.3 %all-to-all-done.1 = bf16[16,32,2048]{2,1,0:T(8,128)(2,1)} async-done(((bf16[16,32,2048]{2,1,0:T(8,128)(2,1)}), bf16[16,32,2048]{2,1,0:T(8,128)(2,1)}, u32[]{:S(2)}, u32[]{:S(2)}) %all-to-all-start.1) | async-done | bytes 2097184 | tf_op jit(solution)/shard_map/all_to_all | solution.py:89
  308.9 4.2 %gather_fusion.1 = bf16[256,2048]{1,0:T(8,128)(2,1)S(1)} fusion(bf16[512,2048]{1,0:T(8,128)(2,1)} %bitcast.10, s32[1024]{0:T(1024)S(1)} %pad_clamp_fusion.1), kind=kCustom, calls=%fused_computation.1 | custom fusion | bytes 2098176 | tf_op jit(solution)/shard_map/gather | solution.py:96
  313.1 1.3 reshape.148
  314.5 6.0 %multiply_reduce_fusion = (f32[128,2]{1,0:T(8,128)S(1)}, bf16[128,2048]{1,0:T(8,128)(2,1)}) fusion(f32[128,2,2048]{2,1,0:T(2,128)S(1)} %reshape.148, f32[128,2048]{1,0:T(8,128)} %convert_element_type.63, f32[128,2]{1,0:T(8,128)S(1)} %copy.29), kind=kLoop, calls=%fused_computation.22 | loop fusion | flops 1834752 | bytes 3672064 | tf_op jit(solution)/shard_map/reduce_sum | solution.py:101
  (57 shorter events, 5.1 us)
Async XLA Ops:
  10.3 2.5 copy-start.4
  10.3 3.8 %copy-start.3 = (s32[128,2]{0,1:T(2,128)S(1)}, s32[128,2]{0,1:T(2,128)}, u32[]{:S(2)}) copy-start(s32[128,2]{0,1:T(2,128)} %param.9) | copy-start | bytes 3076
  21.1 37.3 %all-to-all-start.2 = ((bf16[16,32,2048]{2,1,0:T(8,128)(2,1)}), bf16[16,32,2048]{2,1,0:T(8,128)(2,1)S(1)}, u32[]{:S(2)}, u32[]{:S(2)}) async-start(bf16[16,32,2048]{2,1,0:T(8,128)(2,1)} %bitcast.11), calls=%async_computation.2 | async-start | bytes 4194304 | tf_op jit(solution)/shard_map/all_to_all | solution.py:74
  58.4 4.7 %copy-start.1 = (bf16[16,32,2048]{2,1,0:T(8,128)(2,1)}, bf16[16,32,2048]{2,1,0:T(8,128)(2,1)S(1)}, u32[]{:S(2)}) copy-start(bf16[16,32,2048]{2,1,0:T(8,128)(2,1)S(1)} %all-to-all-done.2) | copy-start | bytes 6291460
  58.4 31.2 %all-to-all-start = ((bf16[16,32,2048]{2,1,0:T(8,128)(2,1)}), bf16[16,32,2048]{2,1,0:T(8,128)(2,1)}, u32[]{:S(2)}, u32[]{:S(2)}) async-start(bf16[16,32,2048]{2,1,0:T(8,128)(2,1)} %bitcast.2), calls=%async_computation | async-start | bytes 4194304 | tf_op jit(solution)/shard_map/all_to_all | solution.py:73
  62.8 109.2 %all-reduce.4.cloned.1.call-start = ((), (), s32[]{:S(2)}) async-start(), calls=%async_computation.4 | async-start | bytes 4194304 | tf_op jit(solution)/shard_map/psum | solution.py:86
  89.5 5.2 %copy-start.6 = (bf16[1,2048,896]{2,1,0:T(8,128)(2,1)S(1)}, bf16[1,2048,896]{2,1,0:T(8,128)(2,1)}, u32[]{:S(2)}) copy-start(bf16[1,2048,896]{2,1,0:T(8,128)(2,1)} %param.11) | copy-start | bytes 11010052
  89.5 5.2 %copy-start.11 = (f32[512,896]{1,0:T(8,128)S(1)}, f32[512,896]{1,0:T(8,128)}, u32[]{:S(2)}) copy-start(f32[512,896]{1,0:T(8,128)} %fusion.2) | copy-start | bytes 5505028
  94.7 4.9 %copy-start.5 = (bf16[1,2048,896]{2,1,0:T(8,128)(2,1)S(1)}, bf16[1,2048,896]{2,1,0:T(8,128)(2,1)}, u32[]{:S(2)}) copy-start(bf16[1,2048,896]{2,1,0:T(8,128)(2,1)} %param.12) | copy-start | bytes 11010052
  99.6 2.4 copy-start.9
  99.6 2.4 copy-start.12
  99.6 6.2 %copy-start.7 = (bf16[512,896]{1,0:T(8,128)(2,1)}, bf16[512,896]{1,0:T(8,128)(2,1)S(1)}, u32[]{:S(2)}) copy-start(bf16[512,896]{1,0:T(8,128)(2,1)S(1)} %get-tuple-element.24) | copy-start | bytes 2752516
  105.7 152.7 %all-gather.3.cloned.1.call-start = ((), (), s32[]{:S(2)}) async-start(), calls=%async_computation.5 | async-start | bytes 18874368 | tf_op jit(solution)/shard_map/all_gather | solution.py:10
  172.0 97.2 %all-to-all-start.3 = ((bf16[16,32,2048]{2,1,0:T(8,128)(2,1)}), bf16[16,32,2048]{2,1,0:T(8,128)(2,1)S(1)}, u32[]{:S(2)}, u32[]{:S(2)}) async-start(bf16[16,32,2048]{2,1,0:T(8,128)(2,1)} %all-reduce.4.cloned.1.call-done), calls=%async_computation.3 | async-start | bytes 4194304 | tf_op jit(solution)/shard_map/all_to_all | solution.py:92
  269.2 7.0 %copy-start = (bf16[128,2048]{1,0:T(8,128)(2,1)S(1)}, bf16[128,2048]{1,0:T(8,128)(2,1)}, u32[]{:S(2)}) copy-start(bf16[128,2048]{1,0:T(8,128)(2,1)} %param.8) | copy-start | bytes 1572868
  269.2 39.7 %all-to-all-start.1 = ((bf16[16,32,2048]{2,1,0:T(8,128)(2,1)}), bf16[16,32,2048]{2,1,0:T(8,128)(2,1)}, u32[]{:S(2)}, u32[]{:S(2)}) async-start(bf16[16,32,2048]{2,1,0:T(8,128)(2,1)} %reduce_sum.52), calls=%async_computation.1 | async-start | bytes 4194304 | tf_op jit(solution)/shard_map/all_to_all | solution.py:89
  277.6 6.1 %copy-start.10 = (bf16[512,896]{1,0:T(8,128)(2,1)S(1)}, bf16[512,896]{1,0:T(8,128)(2,1)}, u32[]{:S(2)}) copy-start(bf16[512,896]{1,0:T(8,128)(2,1)} %copy-done.9) | copy-start | bytes 2752516
  283.7 6.0 %copy-start.2 = (bf16[16,32,2048]{2,1,0:T(8,128)(2,1)S(1)}, bf16[16,32,2048]{2,1,0:T(8,128)(2,1)}, u32[]{:S(2)}) copy-start(bf16[16,32,2048]{2,1,0:T(8,128)(2,1)} %copy-done.1) | copy-start | bytes 6291460
  283.7 6.0 %copy-start.8 = (bf16[512,896]{1,0:T(8,128)(2,1)S(1)}, bf16[512,896]{1,0:T(8,128)(2,1)}, u32[]{:S(2)}) copy-start(bf16[512,896]{1,0:T(8,128)(2,1)} %copy-done.7) | copy-start | bytes 2752516
Sparse Core Ops, SparseCore 0:
  105.9 66.1 all-reduce.3
  174.3 84.1 all-gather.2
